TPU v7x, 512 devices: a whole 4x4x16 slice. The times are simulated.
512 devices in a mesh: dp: 16 (over y_lo, x, core), mp: 32 (over z, y_hi).
Axes of the slice: x: 4, y: 4 (y_hi: 2, y_lo: 2; y = y_hi * 2 + y_lo), z: 16, core: 2. Of those that a mesh axis runs over, the one named last changes fastest.
Arguments:
- hidden_states: bfloat16 [8192, 2560], P(('dp', 'mp')), may hold values from -60 to 60
- norm_gain: float32 [2560], replicated, may hold values from 0.5 to 1.5
- head_weight: bfloat16 [2560, 65536], P(None, ('dp', 'mp')), may hold values from -64 to 64
- target_ids: int32 [8192], P(('dp', 'mp')), may hold values from 0 to 65535
- response_mask: int32 [8192], P(('dp', 'mp')), may hold values from 0 to 1, as said below
Outputs:
- token_logprob: float32 [8192], P(('dp', 'mp'))
- token_entropy: float32 [8192], P(('dp', 'mp'))
Inputs may be any that keep to these rules, and one draw needn't show every extreme that they name: `response_mask`: each aligned run of 256 positions is one rollout: a prompt of 0s, then one span of 1s, then padding 0s.
All inputs are finite; a program needn't handle non-finite values.
Results may differ from a plain program's by a relative error of at most 0.0048.
Values may be sent and summed in bfloat16 or wider, within the bound.
No kernel may reach another device: no remote copies, remote signals or barrier semaphores. Data moves between devices by JAX's collectives and lax.ppermute only.
A program may use at most 64 MiB of HBM per device.

v0:
```python
import jax
import jax.numpy as jnp
from jax import lax
from jax.sharding import PartitionSpec as P

id_base = 256


def local(hidden_states, norm_gain, head_weight, target_ids, response_mask):
    states = hidden_states.astype(jnp.float32)
    mean_square = jnp.mean(states * states, axis=1, keepdims=True)
    normed = (states * lax.rsqrt(mean_square + 1e-06) * norm_gain[None, :]).astype(jnp.bfloat16)
    width = normed.shape[1]
    mp_count = lax.axis_size("mp")
    mp_index = lax.axis_index("mp")
    shard_cols = head_weight.shape[1]
    send_count = normed.shape[0]
    id_high = (target_ids // id_base).astype(jnp.bfloat16)
    id_low = (target_ids % id_base).astype(jnp.bfloat16)
    packed = jnp.concatenate([normed, id_high[:, None], id_low[:, None]], axis=1)
    group = lax.all_gather(packed, "mp", axis=0, tiled=True)
    group_states = group[:, :width]
    group_targets = group[:, width].astype(jnp.int32) * id_base + group[:, width + 1].astype(
        jnp.int32
    )
    column_piece = lax.all_gather(head_weight, "dp", axis=1, tiled=True)
    positions = jnp.arange(column_piece.shape[1], dtype=jnp.int32)
    owners = positions // shard_cols
    column_ids = (owners * mp_count + mp_index) * shard_cols + positions % shard_cols
    logits = jnp.dot(group_states, column_piece, preferred_element_type=jnp.float32)
    top = jnp.max(logits, axis=1)
    shifted = jnp.exp(logits - top[:, None])
    total = jnp.sum(shifted, axis=1)
    moment = jnp.sum(shifted * logits, axis=1)
    hit = group_targets[:, None] == column_ids[None, :]
    chosen = jnp.sum(jnp.where(hit, logits, 0.0), axis=1)
    part_lse = top + jnp.log(total)
    part_expected = moment / total
    stats = jnp.stack([part_lse, part_expected, chosen], axis=0)
    stats = stats.reshape(3, mp_count, send_count)
    got = lax.all_to_all(stats, "mp", split_axis=1, concat_axis=1, tiled=True)
    lse_parts, expected_parts, chosen_parts = (got[0], got[1], got[2])
    top_lse = jnp.max(lse_parts, axis=0)
    log_total = top_lse + jnp.log(jnp.sum(jnp.exp(lse_parts - top_lse[None, :]), axis=0))
    weights = jnp.exp(lse_parts - log_total[None, :])
    expected = jnp.sum(weights * expected_parts, axis=0)
    chosen_logit = jnp.sum(chosen_parts, axis=0)
    scored = response_mask.astype(jnp.float32)
    return ((chosen_logit - log_total) * scored, (log_total - expected) * scored)


def solution(mesh):
    return jax.shard_map(
        local,
        mesh=mesh,
        in_specs=(
            P(("dp", "mp"), None),
            P(),
            P(None, ("dp", "mp")),
            P(("dp", "mp")),
            P(("dp", "mp")),
        ),
        out_specs=(P(("dp", "mp")), P(("dp", "mp"))),
        check_vma=False,
    )
```

profile of v0, /device:TPU:2, one launch (start us, length us, event | category | flops | bytes accessed | tf_op | source)
XLA Modules:
  0.0 291.5 jit_solution(14386886251495838894)
XLA Ops:
  7.2 0.0 all-gather.3.cloned.1.call-start
  7.2 0.7 fusion.18
  7.9 0.1 copy.11
  8.0 0.1 copy.12
  8.1 1.0 fusion.3
  9.1 1.0 fusion.5
  10.1 0.7 concatenate.4
  10.8 0.0 all-gather.3.cloned.1.call-update
  10.8 0.0 all-gather.5.cloned.1.call-start
  10.9 0.7 all-gather.5.cloned.1.call-update
  11.6 158.5 %all-gather.3.cloned.1.call-done = bf16[512,2562]{1,0:T(8,128)(2,1)} async-done(((bf16[16,2562]{1,0:T(8,128)(2,1)}), bf16[512,2562]{1,0:T(8,128)(2,1)}) %all-gather.3.cloned.1.call-update) | async-done | bytes 2623504 | tf_op jit(solution)/shard_map/all_gather | solution.py:21
  170.1 1.2 add_reduce_fusion
  171.3 71.3 %all-gather.5.cloned.1.call-done = bf16[2560,2048]{1,0:T(8,128)(2,1)} async-done(((bf16[2560,128]{1,0:T(8,128)(2,1)}), bf16[2560,2048]{1,0:T(8,128)(2,1)}) %all-gather.5.cloned.1.call-update) | async-done | bytes 10485776 | tf_op jit(solution)/shard_map/all_gather | solution.py:26
  242.6 9.2 %fusion.20 = (f32[512]{0:T(512)S(1)}, f32[512,2048]{1,0:T(8,128)S(1)}) fusion(bf16[2560,2048]{1,0:T(8,128)(2,1)} %all-gather.5.cloned.1.call-done, bf16[512,2562]{1,0:T(8,128)(2,1)} %all-gather.3.cloned.1.call-done), kind=kOutput, calls=%fused_computation.45 | convolution fusion | flops 5369757184 | bytes 17303552 | tf_op jit(solution)/shard_map/dot_general | solution.py:30
  251.8 0.0 copy-start
  251.8 1.8 fusion
  253.7 0.1 add.75
  253.8 0.1 div.43
  253.9 0.1 stack.8
  254.0 29.5 %all_to_all.5 = f32[3,32,16]{2,0,1:T(4,128)S(1)} all-to-all(f32[3,32,16]{2,0,1:T(4,128)S(1)} %copy.13), channel_id=1, replica_groups=mesh['dp'=16,'mp'=32] {'mp'}, dimensions={1} | all-to-all | bytes 12288 | tf_op jit(solution)/shard_map/all_to_all | solution.py:41
  283.5 0.1 fusion.19
  283.6 0.0 copy-done
  283.6 0.5 convert_multiply_fusion.2
  284.1 0.5 subtract_multiply_fusion
  (8 shorter events, 0.2 us)
Async XLA Ops:
  7.2 163.0 %all-gather.3.cloned.1.call-start = ((), (), s32[]{:S(2)}) async-start(), calls=%async_computation.1 | async-start | bytes 2838528 | tf_op jit(solution)/shard_map/all_gather | solution.py:21
  10.8 231.8 %all-gather.5.cloned.1.call-start = ((), (), s32[]{:S(2)}) async-start(), calls=%async_computation.2 | async-start | bytes 11141120 | tf_op jit(solution)/shard_map/all_gather | solution.py:26
  251.8 31.7 %copy-start = (s32[16]{0:T(128)S(1)}, s32[16]{0:T(128)}, u32[]{:S(2)}) copy-start(s32[16]{0:T(128)} %param.9) | copy-start | bytes 196
Sparse Core Ops, SparseCore 0:
  11.1 158.9 all-gather.2
  172.2 70.3 all-gather.4
where the time goes:
time: 292 us; the launch traced here: 291 us
  waiting for transfers between devices  230 us (79%)
  blocking collectives  29.5 us (10%)
  between operations  14.1 us (5%)
  matrix products  9.23 us (3%)
  other arithmetic  6.95 us (2%)
    all_gather x1, waiting for transfers between devices, local(): group = lax.all_gather(packed, 'mp', axis=0, tiled=True)  159 us
    all_gather x1, waiting for transfers between devices, local(): column_piece = lax.all_gather(head_weight, 'dp', axis=1, tiled=True)  71.3 us
    all_to_all x1, blocking collectives, local(): got = lax.all_to_all(stats, 'mp', split_axis=1, concat_axis=1, tiled=True)  29.5 us
    dot_general x1, matrix products, local(): jnp.dot(group_states, column_piece, preferred_element_type=jnp.float32)  9.23 us
  transfers between devices with their start and end apart: 2, of which 2 were waited for; matrix products, arithmetic and copies ran while one was open for 0% of the time, Pallas kernels for 0%

commit v1 on v0

--- a/solution.py
+++ b/solution.py
@@ -38,7 +38,9 @@
     part_expected = moment / total
     stats = jnp.stack([part_lse, part_expected, chosen], axis=0)
     stats = stats.reshape(3, mp_count, send_count)
-    got = lax.all_to_all(stats, "mp", split_axis=1, concat_axis=1, tiled=True)
+    got = jnp.concatenate(
+        lax.all_to_all(jnp.stack(jnp.split(stats, lax.axis_size("mp"), axis=1)), "mp", 0, 0), axis=1
+    )
     lse_parts, expected_parts, chosen_parts = (got[0], got[1], got[2])
     top_lse = jnp.max(lse_parts, axis=0)
     log_total = top_lse + jnp.log(jnp.sum(jnp.exp(lse_parts - top_lse[None, :]), axis=0))

time: 292 us -> 292 us (level)
  the two profiles are of different devices: /device:TPU:2 before, /device:TPU:1 now
where the time goes in v1:
time: 292 us; the launch traced here: 291 us
  waiting for transfers between devices  233 us (80%)
  blocking collectives  27.1 us (9%)
  between operations  14.1 us (5%)
  matrix products  9.23 us (3%)
  other arithmetic  6.94 us (2%)
    all_gather x1, waiting for transfers between devices, local(): group = lax.all_gather(packed, 'mp', axis=0, tiled=True)  149 us
    all_gather x1, waiting for transfers between devices, local(): column_piece = lax.all_gather(head_weight, 'dp', axis=1, tiled=True)  82.5 us
    all_to_all x1, blocking collectives, local(): lax.all_to_all(jnp.stack(jnp.split(stats, lax.axis_size('mp'), axis=1)),...  27.1 us
    dot_general x1, matrix products, local(): jnp.dot(group_states, column_piece, preferred_element_type=jnp.float32)  9.23 us
  transfers between devices with their start and end apart: 2, of which 2 were waited for; matrix products, arithmetic and copies ran while one was open for 0% of the time, Pallas kernels for 0%

profile of v1, /device:TPU:1, one launch (start us, length us, event | category | flops | bytes accessed | tf_op | source)
XLA Modules:
  0.0 291.4 jit_solution(6846925871470071664)
XLA Ops:
  7.2 0.0 all-gather.3.cloned.1.call-start
  7.2 0.7 fusion.18
  7.9 0.1 copy.17
  8.0 0.1 copy.18
  8.1 1.0 fusion.3
  9.1 1.0 fusion.5
  10.1 0.7 concatenate.4
  10.8 0.0 all-gather.3.cloned.1.call-update
  10.8 0.0 all-gather.5.cloned.1.call-start
  10.9 0.7 all-gather.5.cloned.1.call-update
  11.6 149.3 %all-gather.3.cloned.1.call-done = bf16[512,2562]{1,0:T(8,128)(2,1)} async-done(((bf16[16,2562]{1,0:T(8,128)(2,1)}), bf16[512,2562]{1,0:T(8,128)(2,1)}) %all-gather.3.cloned.1.call-update) | async-done | bytes 2623504 | tf_op jit(solution)/shard_map/all_gather | solution.py:21
  160.9 1.2 add_reduce_fusion
  162.1 82.5 %all-gather.5.cloned.1.call-done = bf16[2560,2048]{1,0:T(8,128)(2,1)} async-done(((bf16[2560,128]{1,0:T(8,128)(2,1)}), bf16[2560,2048]{1,0:T(8,128)(2,1)}) %all-gather.5.cloned.1.call-update) | async-done | bytes 10485776 | tf_op jit(solution)/shard_map/all_gather | solution.py:26
  244.6 9.2 %fusion.21 = (f32[512]{0:T(512)S(1)}, f32[512,2048]{1,0:T(8,128)S(1)}) fusion(bf16[2560,2048]{1,0:T(8,128)(2,1)} %all-gather.5.cloned.1.call-done, bf16[512,2562]{1,0:T(8,128)(2,1)} %all-gather.3.cloned.1.call-done), kind=kOutput, calls=%fused_computation.80 | convolution fusion | flops 5369757184 | bytes 17303552 | tf_op jit(solution)/shard_map/dot_general | solution.py:30
  253.9 1.9 multiply_reduce_fusion
  255.8 0.1 add.75
  255.8 0.1 div.43
  255.9 0.1 stack.107
  256.1 0.1 stack.141
  256.2 0.1 copy.19
  256.3 27.1 %all_to_all.5 = f32[32,3,1,16]{3,2,1,0:T(1,128)S(1)} all-to-all(f32[32,3,1,16]{3,2,1,0:T(1,128)S(1)} %copy.19), channel_id=1, replica_groups=mesh['dp'=16,'mp'=32] {'mp'}, dimensions={0} | all-to-all | bytes 12288 | tf_op jit(solution)/shard_map/all_to_all | solution.py:42
  283.3 0.1 fusion.19
  283.5 0.5 convert_multiply_fusion.2
  284.0 0.5 subtract_multiply_fusion
  (13 shorter events, 0.2 us)
Async XLA Ops:
  7.2 153.8 %all-gather.3.cloned.1.call-start = ((), (), s32[]{:S(2)}) async-start(), calls=%async_computation.1 | async-start | bytes 2838528 | tf_op jit(solution)/shard_map/all_gather | solution.py:21
  10.8 233.8 %all-gather.5.cloned.1.call-start = ((), (), s32[]{:S(2)}) async-start(), calls=%async_computation.2 | async-start | bytes 11141120 | tf_op jit(solution)/shard_map/all_gather | solution.py:26
  253.9 29.6 %copy-start = (s32[16]{0:T(128)S(1)}, s32[16]{0:T(128)}, u32[]{:S(2)}) copy-start(s32[16]{0:T(128)} %param.9) | copy-start | bytes 196
Sparse Core Ops, SparseCore 0:
  11.1 149.7 all-gather.2
  163.0 81.5 all-gather.4

commit v2 on v0

--- a/solution.py
+++ b/solution.py
@@ -23,7 +23,9 @@
     group_targets = group[:, width].astype(jnp.int32) * id_base + group[:, width + 1].astype(
         jnp.int32
     )
-    column_piece = lax.all_gather(head_weight, "dp", axis=1, tiled=True)
+    column_piece = jnp.concatenate(
+        lax.all_to_all(jnp.stack([head_weight] * lax.axis_size("dp")), "dp", 0, 0), axis=1
+    )
     positions = jnp.arange(column_piece.shape[1], dtype=jnp.int32)
     owners = positions // shard_cols
     column_ids = (owners * mp_count + mp_index) * shard_cols + positions % shard_cols

time: 292 us -> 261 us (0.89)
  the two profiles are of different devices: /device:TPU:2 before, /device:TPU:4 now
where the time goes in v2:
time: 261 us; the launch traced here: 260 us
  waiting for transfers between devices  192 us (74%)
  blocking collectives  22.2 us (9%)
  between operations  14.1 us (5%)
  starting transfers between devices  10.6 us (4%)
  matrix products  9.3 us (4%)
  local copies, waits for them, and re-layouts  7.37 us (3%)
  other arithmetic  4.49 us (2%)
    all_gather x1, waiting for transfers between devices, local(): group = lax.all_gather(packed, 'mp', axis=0, tiled=True)  192 us
    all_to_all x1, blocking collectives, local(): got = lax.all_to_all(stats, 'mp', split_axis=1, concat_axis=1, tiled=True)  22.2 us
    all_to_all x1, starting transfers between devices, local(): lax.all_to_all(jnp.stack([head_weight] * lax.axis_size('dp')), 'dp', 0, 0)  10.6 us
    dot_general x1, matrix products, local(): jnp.dot(group_states, column_piece, preferred_element_type=jnp.float32)  9.3 us
  transfers between devices with their start and end apart: 2, of which 1 were waited for; matrix products, arithmetic and copies ran while one was open for 1% of the time, Pallas kernels for 0%

profile of v2, /device:TPU:4, one launch (start us, length us, event | category | flops | bytes accessed | tf_op | source)
XLA Modules:
  0.0 260.4 jit_solution(5523966106459552576)
XLA Ops:
  7.2 1.3 copy.14
  8.5 4.8 %stack.6 = bf16[16,2560,128]{1,2,0:T(8,128)(2,1)} broadcast(bf16[2560,128]{0,1:T(8,128)(2,1)S(1)} %copy.14), dimensions={1,2} | broadcast | bytes 11141120 | tf_op jit(solution)/shard_map/stack | solution.py:27
  13.4 10.6 %all-to-all-start = ((bf16[16,2560,128]{1,2,0:T(8,128)(2,1)}), bf16[16,2560,128]{1,2,0:T(8,128)(2,1)}, u32[]{:S(2)}, u32[]{:S(2)}) async-start(bf16[16,2560,128]{1,2,0:T(8,128)(2,1)} %stack.6), calls=%async_computation | async-start | bytes 20971520 | tf_op jit(solution)/shard_map/all_to_all | solution.py:27
  23.9 0.0 all-gather.2.cloned.1.call-start
  24.0 0.1 copy.12
  24.1 0.1 copy.13
  24.2 0.1 fusion.3
  24.3 0.0 copy-done.1
  24.3 0.1 fusion.5
  24.4 0.7 concatenate.4
  25.1 0.0 all-gather.2.cloned.1.call-update
  25.2 192.3 %all-gather.2.cloned.1.call-done = bf16[512,2562]{1,0:T(8,128)(2,1)} async-done(((bf16[16,2562]{1,0:T(8,128)(2,1)}), bf16[512,2562]{1,0:T(8,128)(2,1)}) %all-gather.2.cloned.1.call-update) | async-done | bytes 2623504 | tf_op jit(solution)/shard_map/all_gather | solution.py:21
  217.5 1.2 add_reduce_fusion
  218.7 0.0 all-to-all-done
  218.7 9.3 %fusion.20 = (f32[512]{0:T(512)S(1)}, f32[512,2048]{1,0:T(8,128)S(1)}) fusion(bf16[2560,2048]{0,1:T(8,128)(2,1)} %bitcast.3, bf16[512,2562]{1,0:T(8,128)(2,1)} %all-gather.2.cloned.1.call-done), kind=kOutput, calls=%fused_computation.45 | convolution fusion | flops 5369757184 | bytes 17303552 | tf_op jit(solution)/shard_map/dot_general | solution.py:32
  228.0 0.0 copy-start.2
  228.0 1.8 fusion
  229.8 0.1 stack.7
  229.9 0.1 div.43
  230.0 0.1 add.75
  230.1 22.2 %all_to_all.10 = f32[3,32,16]{2,0,1:T(4,128)S(1)} all-to-all(f32[3,32,16]{2,0,1:T(4,128)S(1)} %copy.15), channel_id=1, replica_groups=mesh['dp'=16,'mp'=32] {'mp'}, dimensions={1} | all-to-all | bytes 12288 | tf_op jit(solution)/shard_map/all_to_all | solution.py:43
  252.3 0.1 fusion.19
  252.4 0.5 convert_multiply_fusion.2
  253.0 0.5 subtract_multiply_fusion
  (15 shorter events, 0.2 us)
Async XLA Ops:
  13.3 10.6 %copy-start.3 = (s32[16]{0:T(128)S(1)}, s32[16]{0:T(128)}, u32[]{:S(2)}) copy-start(s32[16]{0:T(128)} %param.8) | copy-start | bytes 196
  13.3 10.8 %copy-start = (bf16[16,2560]{1,0:T(8,128)(2,1)S(1)}, bf16[16,2560]{1,0:T(8,128)(2,1)}, u32[]{:S(2)}) copy-start(bf16[16,2560]{1,0:T(8,128)(2,1)} %param.5) | copy-start | bytes 245764
  13.3 11.0 %copy-start.1 = (f32[2560]{0:T(1024)S(1)}, f32[2560]{0:T(1024)}, u32[]{:S(2)}) copy-start(f32[2560]{0:T(1024)} %param.6) | copy-start | bytes 30724
  13.4 205.3 %all-to-all-start = ((bf16[16,2560,128]{1,2,0:T(8,128)(2,1)}), bf16[16,2560,128]{1,2,0:T(8,128)(2,1)}, u32[]{:S(2)}, u32[]{:S(2)}) async-start(bf16[16,2560,128]{1,2,0:T(8,128)(2,1)} %stack.6), calls=%async_computation | async-start | bytes 20971520 | tf_op jit(solution)/shard_map/all_to_all | solution.py:27
  23.9 193.5 %all-gather.2.cloned.1.call-start = ((), (), s32[]{:S(2)}) async-start(), calls=%async_computation.2 | async-start | bytes 2838528 | tf_op jit(solution)/shard_map/all_gather | solution.py:21
  228.0 24.5 %copy-start.2 = (s32[16]{0:T(128)S(1)}, s32[16]{0:T(128)}, u32[]{:S(2)}) copy-start(s32[16]{0:T(128)} %param.9) | copy-start | bytes 196
Sparse Core Ops, SparseCore 0:
  27.9 189.5 all-gather.1
